TPU v7x, 32 devices: a whole 2x2x4 slice. The times are simulated.
32 devices in a mesh: grp: 2 (over x), cand: 8 (over z, y), seq: 2 (over core).
Axes of the slice: x: 2, y: 2, z: 4, core: 2. Of those that a mesh axis runs over, the one named last changes fastest.
Arguments:
- x_prefix: bfloat16 [8192, 2560], P(('grp', 'cand', 'seq')), parts along dimension 0, may hold values from -6 to 6
- b_prefix: bfloat16 [8192, 128], P(('grp', 'cand', 'seq')), parts along dimension 0, may hold values from -0.5 to 0.5
- code_prefix: int32 [8192, 40], P(('grp', 'cand', 'seq')), parts along dimension 0, may hold values from 0 to 500
- x_cand: bfloat16 [32, 512, 2560], P(('grp', 'cand'), None, 'seq'), parts along dimension 0, may hold values from -6 to 6
- b_cand: bfloat16 [32, 512, 128], P(('grp', 'cand')), parts along dimension 0, may hold values from -0.5 to 0.5
- c_cand: bfloat16 [32, 512, 128], P(('grp', 'cand')), parts along dimension 0, may hold values from -0.5 to 0.5
- code_cand: int32 [32, 512, 40], P(('grp', 'cand'), None, 'seq'), parts along dimension 0, may hold values from 0 to 500
- lengths: int32 [32], P(('grp', 'cand')), parts along dimension 0, may hold values from 1 to 2, as said below
- dy_cand: bfloat16 [32, 512, 2560], P(('grp', 'cand'), None, 'seq'), parts along dimension 0, may hold values from -1.5 to 1.5
Outputs:
- dx_prefix: bfloat16 [8192, 2560], P(('grp', 'cand', 'seq')), parts along dimension 0
- db_prefix: float32 [8192, 128], P(('grp', 'cand', 'seq')), parts along dimension 0
- dx_cand: bfloat16 [32, 512, 2560], P(('grp', 'cand'), None, 'seq'), parts along dimension 0
- db_cand: float32 [32, 512, 128], P(('grp', 'cand'), 'seq'), parts along dimension 0
- dc_cand: float32 [32, 512, 128], P(('grp', 'cand'), 'seq'), parts along dimension 0
There are 2 independent parts, one for each index of `grp`. A program takes and returns all parts, laid end to end along the dimension named above; each array names one. Nothing has to cross between parts.
Inputs may be any that keep to these rules, and one draw needn't show every extreme that they name: lengths count blocks of 256 tokens.
All inputs are finite; a program needn't handle non-finite values.
Results may differ from a plain program's by a relative error of at most 0.0015.
The roundings to bfloat16 on the way count: a program that leaves them out, or rounds other values in their place, can miss the bound.
Values may be sent and summed in bfloat16 or wider, within the bound.
No kernel may reach another device: no remote copies, remote signals or barrier semaphores. Data moves between devices by JAX's collectives and lax.ppermute only.
A program may use at most 256 MiB of HBM per device.

v0:
```python
import jax
import jax.numpy as jnp
from jax import lax
from jax.sharding import PartitionSpec as P

BLOCK = 256


def split_bf16(value):
    high = lax.reduce_precision(value, exponent_bits=8, mantissa_bits=7)
    low = (value - high).astype(jnp.bfloat16)
    return (high.astype(jnp.bfloat16), low)


def shards(x_prefix, b_prefix, code_prefix, x_cand, b_cand, c_cand, code_cand, lengths, dy_cand):
    pre_len, width = x_prefix.shape
    heads_total = code_prefix.shape[1]
    head_size = width // heads_total
    nstate = b_prefix.shape[1]
    cand_dev, cand_len, half_width = x_cand.shape
    half_heads = code_cand.shape[2]
    pre_axes = ("cand", "seq")
    log_prefix = jnp.log1p(-code_prefix.astype(jnp.float32) * 1e-06)
    own_total = jnp.sum(log_prefix, axis=0)
    shard_count = lax.axis_size(pre_axes)
    mine = lax.axis_index(pre_axes)
    shard_at = jnp.arange(shard_count, dtype=jnp.int32)
    lanes = -(-heads_total // 128) * 128
    padded = jnp.pad(own_total, (0, lanes - heads_total))
    rows = jnp.where((shard_at < mine)[:, None], padded[None, :], 0.0)
    rows = jnp.broadcast_to(rows[:, None, :], (shard_count, 8, lanes))
    later_total = lax.psum_scatter(rows, pre_axes, scatter_dimension=0, tiled=True)
    later_total = later_total[0, 0, :heads_total]
    after_local = own_total[None, :] - jnp.cumsum(log_prefix, axis=0)
    weight = jnp.exp(after_local + later_total[None, :])
    weighted_b = (weight[:, :, None] * b_prefix[:, None, :].astype(jnp.float32)).astype(
        jnp.bfloat16
    )
    x_heads = x_prefix.reshape(pre_len, heads_total, head_size)
    state_full = jnp.einsum("jhp,jhn->hpn", x_heads, weighted_b, preferred_element_type=jnp.float32)
    seq_at = lax.axis_index("seq")
    traced_zero = later_total[0] * 0.0
    init_full = lax.psum(state_full, pre_axes) + traced_zero
    init_half = lax.dynamic_slice_in_dim(init_full, seq_at * half_heads, half_heads, 0)
    init_half = init_half.astype(jnp.bfloat16)
    position = jnp.arange(cand_len, dtype=jnp.int32)
    valid_rows = position[None, :] < lengths[:, None] * BLOCK
    g_cand = jnp.where(valid_rows[:, :, None], dy_cand, jnp.zeros_like(dy_cand))
    level_all = jnp.cumsum(jnp.log1p(-code_cand.astype(jnp.float32) * 1e-06), axis=1)
    amplitude = jnp.exp(level_all)
    inverse = jnp.exp(-level_all)
    g_heads = g_cand.reshape(cand_dev, cand_len, half_heads, head_size)
    xc_heads = x_cand.reshape(cand_dev, cand_len, half_heads, head_size)
    scaled_g = g_heads.astype(jnp.float32) * amplitude[:, :, :, None]
    decayed_g, g_low = split_bf16(scaled_g)
    x_high, x_low = split_bf16(xc_heads.astype(jnp.float32) * inverse[:, :, :, None])
    dstate = jnp.einsum("cthp,ctn->hpn", decayed_g, c_cand, preferred_element_type=jnp.float32)
    grad_half = (lax.psum(dstate, "cand") + traced_zero).astype(jnp.bfloat16)
    grad_state = lax.all_gather(grad_half, "seq", axis=0, tiled=True)
    causal = position[:, None] >= position[None, :]
    flat = (cand_dev, cand_len, half_width)

    def pair(left, right):
        return jnp.einsum(
            "ctk,csk->cts",
            left.reshape(flat),
            right.reshape(flat),
            preferred_element_type=jnp.float32,
        )

    weight_sum = pair(decayed_g, x_high) + pair(decayed_g, x_low) + pair(g_low, x_high)
    weight_sum = jnp.where(causal[None], weight_sum, 0.0)
    db_part = jnp.einsum(
        "cts,ctn->csn", weight_sum, c_cand.astype(jnp.float32), precision=lax.Precision.HIGHEST
    )
    dc_part = jnp.einsum(
        "cts,csn->ctn", weight_sum, b_cand.astype(jnp.float32), precision=lax.Precision.HIGHEST
    )
    scores = jnp.einsum("ctn,csn->cts", c_cand, b_cand, preferred_element_type=jnp.float32)
    amp_t = jnp.transpose(amplitude, (0, 2, 1))
    inv_t = jnp.transpose(inverse, (0, 2, 1))
    decay_mat = amp_t[:, :, :, None] * inv_t[:, :, None, :]
    kernel = jnp.where(causal[None, None], scores[:, None] * decay_mat, 0.0).astype(jnp.bfloat16)
    dx_cand = jnp.einsum("chts,cthp->cshp", kernel, g_heads, preferred_element_type=jnp.float32)
    dx_cand = dx_cand.astype(jnp.bfloat16).reshape(flat)
    dc_state = jnp.dot(
        decayed_g.reshape(cand_dev * cand_len, half_width),
        init_half.reshape(half_width, nstate),
        preferred_element_type=jnp.float32,
    )
    dc_total = dc_part + dc_state.reshape(cand_dev, cand_len, nstate)
    db_cand = lax.psum_scatter(db_part, "seq", scatter_dimension=1, tiled=True)
    dc_cand = lax.psum_scatter(dc_total, "seq", scatter_dimension=1, tiled=True)
    dx_prefix = jnp.einsum(
        "jhn,hpn->jhp", weighted_b, grad_state, preferred_element_type=jnp.float32
    )
    dx_prefix = dx_prefix.astype(jnp.bfloat16).reshape(pre_len, width)
    projected = jnp.einsum("jhp,hpn->jhn", x_heads, grad_state, preferred_element_type=jnp.float32)
    db_prefix = jnp.sum(projected * weight[:, :, None], axis=1)
    return (dx_prefix, db_prefix, dx_cand, db_cand, dc_cand)


def solution(mesh):
    return jax.shard_map(
        shards,
        mesh=mesh,
        in_specs=(
            P(("grp", "cand", "seq"), None),
            P(("grp", "cand", "seq"), None),
            P(("grp", "cand", "seq"), None),
            P(("grp", "cand"), None, "seq"),
            P(("grp", "cand"), None, None),
            P(("grp", "cand"), None, None),
            P(("grp", "cand"), None, "seq"),
            P(("grp", "cand")),
            P(("grp", "cand"), None, "seq"),
        ),
        out_specs=(
            P(("grp", "cand", "seq"), None),
            P(("grp", "cand", "seq"), None),
            P(("grp", "cand"), None, "seq"),
            P(("grp", "cand"), "seq", None),
            P(("grp", "cand"), "seq", None),
        ),
        check_vma=False,
    )
```

profile of v0, /device:TPU:0, one launch (start us, length us, event | category | flops | bytes accessed | tf_op | source)
XLA Modules:
  0.0 305.6 jit_solution(1528307880977346940)
XLA Ops:
  7.3 0.9 fusion.26
  8.3 0.6 broadcast_in_dim.84
  9.0 1.0 log-plus-one_bitcast_fusion
  10.0 0.1 reshape.156
  10.1 2.3 reduce-window.14
  12.5 0.2 slice_reduce_fusion
  12.7 0.1 negate_exponential_fusion
  12.8 0.6 reduce-window.16
  13.4 0.2 slice_reduce_fusion.1
  13.6 2.4 copy.63
  16.1 0.1 copy.61
  16.2 0.6 dynamic-slice
  16.8 82.5 %all-reduce.10.cloned.1.call-done = f32[16,8,128]{2,1,0:T(8,128)} async-done(((f32[16,8,128]{2,1,0:T(8,128)}), f32[16,8,128]{2,1,0:T(8,128)}) %all-reduce.10.cloned.1.call-update) | async-done | bytes 65552
  99.3 1.3 constant_dynamic-slice_fusion
  100.6 0.1 fusion.25
  100.7 0.6 copy-done.12
  101.3 3.5 %fusion.19 = f32[40,64,128]{2,1,0:T(8,128)} fusion(bf16[256,40,64]{0,2,1:T(8,128)(2,1)} %bitcast.91, f32[256,128]{0,1:T(8,128)S(1)} %copy.61, f32[256,40]{0,1:T(8,128)S(1)} %fusion.25), kind=kOutput, calls=%fused_computation.31 | convolution fusion | flops 170393600 | bytes 2793472 | tf_op jit(solution)/shard_map/jhp,jhn->hpn/dot_general | solution.py:40
  105.2 2.6 copy.55
  107.9 4.4 %copy.67 = bf16[2,512,1280]{1,2,0:T(8,128)(2,1)} copy(bf16[2,512,1280]{2,1,0:T(8,128)(2,1)} %param.12) | data formatting | bytes 5242880 | tf_op args[3]
  112.4 5.7 %fusion.6 = (bf16[2,512,1280]{1,2,0:T(8,128)(2,1)}, bf16[2,512,1280]{1,2,0:T(8,128)(2,1)S(1)}, bf16[2,512,1280]{1,2,0:T(8,128)(2,1)}, bf16[2,512,1280]{1,2,0:T(8,128)(2,1)}) fusion(f32[2,512,20]{1,2,0:T(8,128)S(1)} %copy.58, bf16[2,512,1280]{1,2,0:T(8,128)(2,1)} %copy.55, pred[2,512]{1,0:T(4,128)(4,1)S(1)} %iota_compare_fusion.1, ...), kind=kLoop, calls=%fused_computation.11 | loop fusion | flops 15728640 | bytes 15893504 | tf_op jit(solution)/shard_map/convert_element_type | solution.py:11
  118.0 1.7 fusion.20
  119.8 0.2 reduce-scatter.3.cloned.1.call-start
  120.0 0.5 reduce-precision_convert_fusion.1
  120.7 1.7 copy-done.5
  122.4 1.6 fusion.30
  124.0 0.2 copy-done.6
  124.2 1.6 fusion.31
  125.8 0.2 copy-done.4
  125.9 1.8 add_select_fusion
  127.7 2.7 fusion.32
  130.4 0.3 reduce-scatter.5.cloned.1.call-start
  130.7 1.8 fusion.29
  132.5 1.9 fusion.33
  134.4 0.5 slice.22
  135.6 64.6 %all-reduce.8.cloned.1.call-done = f32[40,64,128]{2,1,0:T(8,128)} async-done(((f32[40,64,128]{2,1,0:T(8,128)}), f32[40,64,128]{2,1,0:T(8,128)}) %all-reduce.8.cloned.1.call-update) | async-done | bytes 1310736 | tf_op jit(solution)/shard_map/psum | solution.py:43
  200.2 1.3 fusion.21
  201.5 3.5 %convolution_add_fusion = f32[2,512,128]{2,1,0:T(8,128)} fusion(f32[2,512,128]{2,1,0:T(8,128)} %fusion.33, bf16[2,512,1280]{1,2,0:T(8,128)(2,1)} %copy-done.3, bf16[1280,128,1]{1,0,2:T(8,128)(2,1)S(1)} %bitcast.94), kind=kOutput, calls=%fused_computation.33 | convolution fusion | flops 335675392 | bytes 3997696 | tf_op jit(solution)/shard_map/dot_general | solution.py:86
  205.0 7.7 %fusion.17 = bf16[2,20,64,512]{3,2,1,0:T(8,128)(2,1)} fusion(bf16[2,512,20,64]{1,3,2,0:T(8,128)(2,1)S(1)} %bitcast.89, f32[2,20,512]{2,1,0:T(8,128)S(1)} %copy.66, f32[2,20,512]{2,1,0:T(8,128)S(1)} %copy.64, f32[2,512,512]{2,1,0:T(8,128)} %fusion.29, pred[512,512]{1,0:T(8,128)(4,1)S(1)} %iota_compare_fusion), kind=kOutput, calls=%fused_computation.29 | convolution fusion | flops 1385431040 | bytes 7766016 | tf_op jit(solution)/shard_map/chts,cthp->cshp/dot_general | solution.py:84
  212.8 4.4 %copy.80 = bf16[2,512,1280]{2,1,0:T(8,128)(2,1)} copy(bf16[2,512,1280]{1,2,0:T(8,128)(2,1)} %bitcast.90) | data formatting | bytes 5242880
  217.1 60.1 %all-reduce.6.cloned.1.call-done = f32[20,64,128]{2,1,0:T(8,128)} async-done(((f32[20,64,128]{2,1,0:T(8,128)}), f32[20,64,128]{2,1,0:T(8,128)}) %all-reduce.6.cloned.1.call-update) | async-done | bytes 655376 | tf_op jit(solution)/shard_map/psum | solution.py:58
  277.3 1.2 add_convert_fusion
  278.4 2.3 all_gather.3
  280.7 1.5 fusion.18
  282.3 1.6 copy.78
  283.8 1.7 fusion.8
  285.5 0.8 copy.79
  286.3 0.9 reduce-scatter.3.cloned.1.call-done
  287.2 11.9 %reduce-scatter.5.cloned.1.call-done = f32[2,256,128]{2,1,0:T(8,128)} async-done(((f32[2,512,128]{2,1,0:T(8,128)}), f32[2,256,128]{2,1,0:T(8,128)}) %reduce-scatter.5.cloned.1.call-update) | async-done | bytes 262160 | tf_op jit(solution)/shard_map/reduce_scatter | solution.py:93
  (55 shorter events, 0.9 us)
Async XLA Ops:
  7.2 110.9 %copy-start = (bf16[2,512,128]{2,1,0:T(8,128)(2,1)S(1)}, bf16[2,512,128]{2,1,0:T(8,128)(2,1)}, u32[]{:S(2)}) copy-start(bf16[2,512,128]{2,1,0:T(8,128)(2,1)} %param.14) | copy-start | bytes 786436
  7.2 9.0 %copy-start.14 = (u32[32]{0:T(128)S(1)}, u32[32]{0:T(128)}, u32[]{:S(2)}) copy-start(u32[32]{0:T(128)} %constant.44) | copy-start | bytes 388
  7.2 8.9 %copy-start.11 = (bf16[256,128]{1,0:T(8,128)(2,1)S(1)}, bf16[256,128]{1,0:T(8,128)(2,1)}, u32[]{:S(2)}) copy-start(bf16[256,128]{1,0:T(8,128)(2,1)} %param.10) | copy-start | bytes 196612
  7.2 92.1 %all-reduce.10.cloned.1.call-start = ((), (), s32[]{:S(2)}) async-start(), calls=%async_computation.6 | async-start | bytes 131072
  9.0 191.2 %all-reduce.8.cloned.1.call-start = ((), (), s32[]{:S(2)}) async-start(), calls=%async_computation.4 | async-start | bytes 2621440 | tf_op jit(solution)/shard_map/psum | solution.py:43
  16.1 88.9 %copy-start.13 = (s32[2]{0:T(128)S(1)}, s32[2]{0:T(128)}, u32[]{:S(2)}) copy-start(s32[2]{0:T(128)} %param.16) | copy-start | bytes 28
  16.2 88.8 %copy-start.10 = (f32[256,128]{0,1:T(8,128)}, f32[256,128]{0,1:T(8,128)S(1)}, u32[]{:S(2)}) copy-start(f32[256,128]{0,1:T(8,128)S(1)} %copy.61) | copy-start | bytes 393220
  100.7 0.6 copy-start.12
  101.3 3.9 %copy-start.7 = (bf16[2,512,1280]{2,1,0:T(8,128)(2,1)S(1)}, bf16[2,512,1280]{2,1,0:T(8,128)(2,1)}, u32[]{:S(2)}) copy-start(bf16[2,512,1280]{2,1,0:T(8,128)(2,1)} %param.17) | copy-start | bytes 7864324
  104.9 172.4 %all-reduce.6.cloned.1.call-start = ((), (), s32[]{:S(2)}) async-start(), calls=%async_computation.2 | async-start | bytes 1310720 | tf_op jit(solution)/shard_map/psum | solution.py:58
  118.0 2.0 copy-start.1
  119.8 167.4 %reduce-scatter.3.cloned.1.call-start = ((), (), s32[]{:S(2)}) async-start(), calls=%async_computation.3 | async-start | bytes 786432 | tf_op jit(solution)/shard_map/reduce_scatter | solution.py:92
  120.0 2.4 copy-start.5
  120.6 3.4 %copy-start.3 = (bf16[2,512,1280]{1,2,0:T(8,128)(2,1)}, bf16[2,512,1280]{1,2,0:T(8,128)(2,1)S(1)}, u32[]{:S(2)}) copy-start(bf16[2,512,1280]{1,2,0:T(8,128)(2,1)S(1)} %reduce-precision_convert_fusion.1) | copy-start | bytes 7864324
  122.4 1.8 copy-start.6
  124.2 1.7 copy-start.4
  127.7 3.0 copy-start.9
  130.4 168.7 %reduce-scatter.5.cloned.1.call-start = ((), (), s32[]{:S(2)}) async-start(), calls=%async_computation.5 | async-start | bytes 786432 | tf_op jit(solution)/shard_map/reduce_scatter | solution.py:93
  200.2 4.9 %copy-start.2 = (bf16[2,512,1280]{1,2,0:T(8,128)(2,1)S(1)}, bf16[2,512,1280]{1,2,0:T(8,128)(2,1)}, u32[]{:S(2)}) copy-start(bf16[2,512,1280]{1,2,0:T(8,128)(2,1)} %copy-done.1) | copy-start | bytes 7864324
  280.7 3.1 %copy-start.8 = (bf16[256,2560]{0,1:T(8,128)(2,1)S(1)}, bf16[256,2560]{0,1:T(8,128)(2,1)}, u32[]{:S(2)}) copy-start(bf16[256,2560]{0,1:T(8,128)(2,1)} %copy.63) | copy-start | bytes 3932164
Sparse Core Ops, SparseCore 0:
  12.1 87.1 all-reduce.9
  105.0 95.1 all-reduce.7
  204.0 73.2 all-reduce.5
  280.0 7.2 reduce-scatter.2
  290.0 9.0 reduce-scatter.4
where the time goes:
time: 306 us
  waiting for transfers between devices  220 us (72%)
  matrix products  31 us (10%)
  local copies, waits for them, and re-layouts  22.8 us (7%)
  between operations  14.8 us (5%)
  other arithmetic  14 us (5%)
    unnamed x6, waiting for transfers between devices  82.6 us
    psum x1, waiting for transfers between devices, shards(): init_full = lax.psum(state_full, pre_axes) + traced_zero  64.6 us
    psum x1, waiting for transfers between devices, shards(): grad_half = (lax.psum(dstate, 'cand') + traced_zero).astype(jnp.bfloat16)  60.1 us
    unnamed x38, local copies, waits for them, and re-layouts  20.8 us
    reduce_scatter x1, waiting for transfers between devices, shards(): dc_cand = lax.psum_scatter(dc_total, 'seq', scatter_dimension=1, tiled=True)  11.9 us
    dot_general x1, matrix products, shards(): jnp.einsum('chts,cthp->cshp', kernel, g_heads, preferred_element_type=jnp...  7.72 us
  transfers between devices with their start and end apart: 5, of which 5 were waited for; matrix products, arithmetic and copies ran while one was open for 19% of the time, Pallas kernels for 0%

commit v1 on v0

--- a/solution.py
+++ b/solution.py
@@ -40,7 +40,7 @@
     state_full = jnp.einsum("jhp,jhn->hpn", x_heads, weighted_b, preferred_element_type=jnp.float32)
     seq_at = lax.axis_index("seq")
     traced_zero = later_total[0] * 0.0
-    init_full = lax.psum(state_full, pre_axes) + traced_zero
+    init_full = jnp.sum(lax.all_gather(state_full, pre_axes), 0) + traced_zero
     init_half = lax.dynamic_slice_in_dim(init_full, seq_at * half_heads, half_heads, 0)
     init_half = init_half.astype(jnp.bfloat16)
     position = jnp.arange(cand_len, dtype=jnp.int32)

time: 306 us -> 278 us (0.908)
  waiting for transfers between devices: 220 us -> 184 us
  other arithmetic: 14 us -> 22.3 us
  matrix products: 31 us -> 27.7 us
    all_gather x0 -> x1, waiting for transfers between devices: none -> 85 us  [shards(): init_full = jnp.sum(lax.all_gather(state_full, pre_axes), 0) + traced_zero]
    psum x1 -> x0, waiting for transfers between devices: 64.6 us -> none  [shards(): init_full = lax.psum(state_full, pre_axes) + traced_zero]
    psum x1, waiting for transfers between devices: 60.1 us -> 12.7 us  [shards(): grad_half = (lax.psum(dstate, 'cand') + traced_zero).astype(jnp.bfloat16)]
    reduce_scatter x1, waiting for transfers between devices: 11.9 us -> 0.01 us  [shards(): dc_cand = lax.psum_scatter(dc_total, 'seq', scatter_dimension=1, tiled=True)]
    reduce_sum x0 -> x1, other arithmetic: none -> 9.14 us  [shards(): init_full = jnp.sum(lax.all_gather(state_full, pre_axes), 0) + traced_zero]
    unnamed x6, waiting for transfers between devices: 82.6 us -> 86.8 us
    unnamed x38 -> x44, local copies, waits for them, and re-layouts: 20.8 us -> 20 us
  transfers between devices with their start and end apart: 5 -> 5, of which waited for: 5 -> 3; matrix products, arithmetic and copies ran while one was open for 19% -> 24% of each run, Pallas kernels for 0% -> 0%
where the time goes in v1:
time: 278 us; the launch traced here: 277 us
  waiting for transfers between devices  184 us (66%)
  matrix products  27.7 us (10%)
  local copies, waits for them, and re-layouts  23.4 us (8%)
  other arithmetic  22.3 us (8%)
  between operations  16.2 us (6%)
    unnamed x6, waiting for transfers between devices  86.8 us
    all_gather x1, waiting for transfers between devices, shards(): init_full = jnp.sum(lax.all_gather(state_full, pre_axes), 0) + traced_zero  85 us
    unnamed x44, local copies, waits for them, and re-layouts  20 us
    psum x1, waiting for transfers between devices, shards(): grad_half = (lax.psum(dstate, 'cand') + traced_zero).astype(jnp.bfloat16)  12.7 us
    reduce_sum x1, other arithmetic, shards(): init_full = jnp.sum(lax.all_gather(state_full, pre_axes), 0) + traced_zero  9.14 us
    dot_general x1, matrix products, shards(): jnp.einsum('chts,cthp->cshp', kernel, g_heads, preferred_element_type=jnp...  7.72 us
    convert_element_type x1, other arithmetic, split_bf16(): low = (value - high).astype(jnp.bfloat16)  5.66 us
  transfers between devices with their start and end apart: 5, of which 3 were waited for; matrix products, arithmetic and copies ran while one was open for 24% of the time, Pallas kernels for 0%

profile of v1, /device:TPU:0, one launch (start us, length us, event | category | flops | bytes accessed | tf_op | source)
XLA Modules:
  0.0 276.9 jit_solution(2644112052217907883)
XLA Ops:
  8.1 0.9 fusion.26
  9.1 0.6 broadcast_in_dim.84
  9.8 0.6 reduce-window.16
  10.4 0.2 slice_reduce_fusion.1
  10.6 1.0 copy.61
  11.6 1.6 copy.63
  13.2 0.6 dynamic-slice
  13.8 86.7 %all-reduce.7.cloned.1.call-done = f32[16,8,128]{2,1,0:T(8,128)} async-done(((f32[16,8,128]{2,1,0:T(8,128)}), f32[16,8,128]{2,1,0:T(8,128)}) %all-reduce.7.cloned.1.call-update) | async-done | bytes 65552
  100.5 1.3 constant_dynamic-slice_fusion
  101.8 0.1 fusion.25
  101.9 2.1 fusion.19
  104.1 0.1 log-plus-one_bitcast_fusion
  104.3 0.1 reshape.156
  104.4 2.3 reduce-window.14
  106.7 0.2 slice_reduce_fusion
  106.9 0.1 negate_exponential_fusion
  107.3 2.7 copy.67
  110.0 4.6 %copy.55 = bf16[2,512,1280]{1,2,0:T(8,128)(2,1)} copy(bf16[2,512,1280]{2,1,0:T(8,128)(2,1)} %param.17) | data formatting | bytes 5242880 | tf_op args[8]
  114.6 5.7 %fusion.6 = (bf16[2,512,1280]{1,2,0:T(8,128)(2,1)}, bf16[2,512,1280]{1,2,0:T(8,128)(2,1)S(1)}, bf16[2,512,1280]{1,2,0:T(8,128)(2,1)}, bf16[2,512,1280]{1,2,0:T(8,128)(2,1)}) fusion(f32[2,512,20]{1,2,0:T(8,128)S(1)} %copy.58, bf16[2,512,1280]{1,2,0:T(8,128)(2,1)} %copy.55, pred[2,512]{1,0:T(4,128)(4,1)S(1)} %iota_compare_fusion.1, ...), kind=kLoop, calls=%fused_computation.11 | loop fusion | flops 15728640 | bytes 15893504 | tf_op jit(solution)/shard_map/convert_element_type | solution.py:11
  120.3 1.7 fusion.20
  122.1 0.2 reduce-scatter.3.cloned.1.call-start
  122.3 0.1 iota_compare_fusion
  122.4 0.5 reduce-precision_convert_fusion.1
  123.0 1.9 copy-done.7
  124.8 1.6 fusion.31
  126.4 0.2 copy-done.6
  126.6 1.6 fusion.30
  128.2 0.2 copy-done.5
  128.4 1.8 add_select_fusion
  130.2 2.7 fusion.32
  132.9 0.3 reduce-scatter.5.cloned.1.call-start
  133.2 0.7 copy.66
  133.8 1.8 fusion.29
  135.6 1.9 fusion.33
  137.5 0.5 slice.22
  138.6 85.0 %all-gather.3.cloned.1.call-done = f32[640,64,128]{2,1,0:T(8,128)} async-done(((f32[40,64,128]{2,1,0:T(8,128)}), f32[640,64,128]{2,1,0:T(8,128)}) %all-gather.3.cloned.1.call-update) | async-done | bytes 20971536 | tf_op jit(solution)/shard_map/all_gather | solution.py:43
  223.6 9.1 %reduce_sum.29 = f32[40,64,128]{2,1,0:T(8,128)} reduce(f32[16,40,64,128]{3,2,1,0:T(8,128)} %bitcast.89, f32[]{:T(128)} %constant.14.clone.1), dimensions={0}, to_apply=%region_9.10 | reduce | flops 4915200 | bytes 22282244 | tf_op jit(solution)/shard_map/reduce_sum | solution.py:43
  232.7 1.3 fusion.21
  234.1 3.6 %convolution_add_fusion = f32[2,512,128]{2,1,0:T(8,128)} fusion(f32[2,512,128]{2,1,0:T(8,128)} %fusion.33, bf16[2,512,1280]{1,2,0:T(8,128)(2,1)} %copy-done.4, bf16[1280,128,1]{1,0,2:T(8,128)(2,1)S(1)} %bitcast.96), kind=kOutput, calls=%fused_computation.33 | convolution fusion | flops 335675392 | bytes 3997696 | tf_op jit(solution)/shard_map/dot_general | solution.py:86
  237.6 7.7 %fusion.17 = bf16[2,20,64,512]{3,2,1,0:T(8,128)(2,1)} fusion(bf16[2,512,20,64]{1,3,2,0:T(8,128)(2,1)S(1)} %bitcast.91, f32[2,20,512]{2,1,0:T(8,128)S(1)} %copy-done.12, f32[2,20,512]{2,1,0:T(8,128)S(1)} %copy.64, f32[2,512,512]{2,1,0:T(8,128)} %fusion.29, pred[512,512]{1,0:T(8,128)(4,1)S(1)} %iota_compare_fusion), kind=kOutput, calls=%fused_computation.29 | convolution fusion | flops 1385431040 | bytes 7766016 | tf_op jit(solution)/shard_map/chts,cthp->cshp/dot_general | solution.py:84
  245.4 4.5 %copy.80 = bf16[2,512,1280]{2,1,0:T(8,128)(2,1)} copy(bf16[2,512,1280]{1,2,0:T(8,128)(2,1)} %bitcast.92) | data formatting | bytes 5242880
  249.9 12.7 %all-reduce.5.cloned.1.call-done = f32[20,64,128]{2,1,0:T(8,128)} async-done(((f32[20,64,128]{2,1,0:T(8,128)}), f32[20,64,128]{2,1,0:T(8,128)}) %all-reduce.5.cloned.1.call-update) | async-done | bytes 655376 | tf_op jit(solution)/shard_map/psum | solution.py:58
  262.6 1.2 add_convert_fusion
  263.7 2.3 all_gather.9
  266.0 0.9 fusion.8
  266.9 0.8 copy.79
  267.7 0.5 fusion.18
  268.2 1.6 copy.78
  (62 shorter events, 0.8 us)
Async XLA Ops:
  8.0 112.3 %copy-start = (bf16[2,512,128]{2,1,0:T(8,128)(2,1)S(1)}, bf16[2,512,128]{2,1,0:T(8,128)(2,1)}, u32[]{:S(2)}) copy-start(bf16[2,512,128]{2,1,0:T(8,128)(2,1)} %param.14) | copy-start | bytes 786436
  8.0 5.2 %copy-start.17 = (u32[32]{0:T(128)S(1)}, u32[32]{0:T(128)}, u32[]{:S(2)}) copy-start(u32[32]{0:T(128)} %constant.44) | copy-start | bytes 388
  8.0 92.5 %all-reduce.7.cloned.1.call-start = ((), (), s32[]{:S(2)}) async-start(), calls=%async_computation.6 | async-start | bytes 131072
  9.8 213.8 %all-gather.3.cloned.1.call-start = ((), (), s32[]{:S(2)}) async-start(), calls=%async_computation.5 | async-start | bytes 22282240 | tf_op jit(solution)/shard_map/all_gather | solution.py:43
  13.2 88.7 %copy-start.9 = (bf16[256,2560]{0,1:T(8,128)(2,1)}, bf16[256,2560]{0,1:T(8,128)(2,1)S(1)}, u32[]{:S(2)}) copy-start(bf16[256,2560]{0,1:T(8,128)(2,1)S(1)} %copy.63) | copy-start | bytes 3932164
  13.2 90.9 %copy-start.13 = (s32[2,512,20]{1,0,2:T(2,128)S(1)}, s32[2,512,20]{1,0,2:T(2,128)}, u32[]{:S(2)}) copy-start(s32[2,512,20]{1,0,2:T(2,128)} %param.15) | copy-start | bytes 245764
  101.9 2.1 copy-start.14
  104.0 3.3 %copy-start.8 = (bf16[2,512,1280]{2,1,0:T(8,128)(2,1)S(1)}, bf16[2,512,1280]{2,1,0:T(8,128)(2,1)}, u32[]{:S(2)}) copy-start(bf16[2,512,1280]{2,1,0:T(8,128)(2,1)} %param.12) | copy-start | bytes 7864324
  104.1 158.5 %all-reduce.5.cloned.1.call-start = ((), (), s32[]{:S(2)}) async-start(), calls=%async_computation.2 | async-start | bytes 1310720 | tf_op jit(solution)/shard_map/psum | solution.py:58
  110.0 4.6 %copy-start.16 = (s32[2]{0:T(128)S(1)}, s32[2]{0:T(128)}, u32[]{:S(2)}) copy-start(s32[2]{0:T(128)} %param.16) | copy-start | bytes 28
  120.3 2.1 copy-start.2
  122.1 147.7 %reduce-scatter.3.cloned.1.call-start = ((), (), s32[]{:S(2)}) async-start(), calls=%async_computation.3 | async-start | bytes 786432 | tf_op jit(solution)/shard_map/reduce_scatter | solution.py:92
  122.4 2.4 copy-start.7
  122.9 3.5 %copy-start.4 = (bf16[2,512,1280]{1,2,0:T(8,128)(2,1)}, bf16[2,512,1280]{1,2,0:T(8,128)(2,1)S(1)}, u32[]{:S(2)}) copy-start(bf16[2,512,1280]{1,2,0:T(8,128)(2,1)S(1)} %reduce-precision_convert_fusion.1) | copy-start | bytes 7864324
  124.8 1.8 copy-start.6
  126.6 1.8 copy-start.5
  130.2 3.6 %copy-start.11 = (bf16[2,512,128]{2,1,0:T(8,128)(2,1)S(1)}, bf16[2,512,128]{2,1,0:T(8,128)(2,1)}, u32[]{:S(2)}) copy-start(bf16[2,512,128]{2,1,0:T(8,128)(2,1)} %param.13) | copy-start | bytes 786436
  132.9 136.9 %reduce-scatter.5.cloned.1.call-start = ((), (), s32[]{:S(2)}) async-start(), calls=%async_computation.4 | async-start | bytes 786432 | tf_op jit(solution)/shard_map/reduce_scatter | solution.py:93
  232.7 4.9 %copy-start.3 = (bf16[2,512,1280]{1,2,0:T(8,128)(2,1)S(1)}, bf16[2,512,1280]{1,2,0:T(8,128)(2,1)}, u32[]{:S(2)}) copy-start(bf16[2,512,1280]{1,2,0:T(8,128)(2,1)} %copy-done.2) | copy-start | bytes 7864324
  232.7 4.9 %copy-start.12 = (f32[2,20,512]{2,1,0:T(8,128)S(1)}, f32[2,20,512]{2,1,0:T(8,128)}, u32[]{:S(2)}) copy-start(f32[2,20,512]{2,1,0:T(8,128)} %copy.66) | copy-start | bytes 245764
  245.4 20.6 %copy-start.10 = (bf16[256,2560]{0,1:T(8,128)(2,1)S(1)}, bf16[256,2560]{0,1:T(8,128)(2,1)}, u32[]{:S(2)}) copy-start(bf16[256,2560]{0,1:T(8,128)(2,1)} %copy-done.9) | copy-start | bytes 3932164
  245.4 20.6 %copy-start.15 = (f32[256,40]{0,1:T(8,128)S(1)}, f32[256,40]{0,1:T(8,128)}, u32[]{:S(2)}) copy-start(f32[256,40]{0,1:T(8,128)} %copy-done.14) | copy-start | bytes 122884
  266.0 3.8 %copy-start.1 = (bf16[2,512,128]{2,1,0:T(8,128)(2,1)S(1)}, bf16[2,512,128]{2,1,0:T(8,128)(2,1)}, u32[]{:S(2)}) copy-start(bf16[2,512,128]{2,1,0:T(8,128)(2,1)} %param.14) | copy-start | bytes 786436
Sparse Core Ops, SparseCore 0:
  13.3 87.1 all-reduce.6
  104.2 119.3 all-gather.2
  226.4 8.2 reduce-scatter.2
  237.8 8.7 reduce-scatter.4
Sparse Core Ops, SparseCore 1:
  122.1 140.4 all-reduce.4
